TPU v7x, 256 devices: a whole 4x4x8 slice. The times are simulated.
256 devices in a mesh: gx: 4 (over z_lo), gy: 8 (over z_hi, y), gz: 8 (over x, core).
Axes of the slice: x: 4, y: 4, z: 8 (z_hi: 2, z_lo: 4; z = z_hi * 4 + z_lo), core: 2. Of those that a mesh axis runs over, the one named last changes fastest.
Arguments:
- vectors: float32 [4, 5, 125, 4, 8, 1024], P(None, None, None, 'gx', 'gy', 'gz'), may hold values from -6 to 6
- stiffness: float32 [5, 5], replicated, may hold values from -2.5 to 2.5
- flux: float32 [3, 5, 5], replicated, may hold values from -1.25 to 1.25
- penalty: float32 [3, 5], replicated, may hold values from 0.2 to 2
- local_factor: float32 [5, 5], replicated, may hold values from -2.5 to 2.5
- element_field_factor: float32 [5, 5], replicated, may hold values from -2.5 to 2.5
- aggregate: int32 [4, 8, 1024], P('gx', 'gy', 'gz'), may hold values from 0 to 1023
- coarse_inverse: float32 [20480, 5120], P(('gx', 'gy', 'gz')), may hold values from -0.078125 to 0.078125
Outputs:
- result: float32 [4, 5, 125, 4, 8, 1024], P(None, None, None, 'gx', 'gy', 'gz')
Inputs may be any that keep to these rules, and one draw needn't show every extreme that they name: aggregate numbers are counted within the elements of one index of gx.
All inputs are finite; a program needn't handle non-finite values.
Results may differ from a plain program's by a relative error of at most 0.0001.
Values sent between devices are 32-bit elements; how exact they have to be, the bound alone decides.
No kernel may reach another device: no remote copies, remote signals or barrier semaphores. Data moves between devices by JAX's collectives and lax.ppermute only.
A program may use at most 256 MiB of HBM per device.

v0:
```python
import jax
import jax.numpy as jnp
import numpy as np
from jax import lax
from jax.sharding import PartitionSpec as P

HIGH = lax.Precision.HIGHEST


def with_halo(shard, sides, width):
    for axis, dim in sides:
        size, length = (lax.axis_size(axis), shard.shape[dim])
        up = [(i, (i + 1) % size) for i in range(size - 1)]
        down = [(j, i) for i, j in up]
        last = lax.slice_in_dim(shard, length - width, length, axis=dim)
        initial = lax.slice_in_dim(shard, 0, width, axis=dim)
        before = lax.ppermute(last, axis, up)
        after = lax.ppermute(initial, axis, down)
        shard = jnp.concatenate([before, shard, after], axis=dim)
    return shard


def kron_three(first, second, third):
    return jnp.kron(jnp.kron(first, second), third)


def operator_matrix(stiffness, flux):
    unit = jnp.eye(5, dtype=jnp.float32)
    sweeps = [
        kron_three(stiffness, unit, unit),
        kron_three(unit, stiffness, unit),
        kron_three(unit, unit, stiffness),
    ]
    total = jnp.zeros((625, 625), jnp.float32)
    for axis in range(3):
        total = total + jnp.kron(flux[axis], sweeps[axis])
    return total.reshape(5, 125, 5, 125)


def face_table():
    table = np.zeros((150, 125), np.float32)
    for axis in range(3):
        for side in range(2):
            level = 4 * side
            for first in range(5):
                for second in range(5):
                    if axis == 0:
                        node = 25 * level + 5 * first + second
                    elif axis == 1:
                        node = 25 * first + 5 * level + second
                    else:
                        node = 25 * first + 5 * second + level
                    table[50 * axis + 25 * side + 5 * first + second, node] = 1.0
    return table


def operate(flat, dims, big, penalty, selects):
    vecs, fields, elements = (flat.shape[0], flat.shape[1], flat.shape[3])
    output = flat + jnp.einsum("fqgp,kgpe->kfqe", big, flat, precision=HIGH)
    faces = jnp.einsum("sq,kfqe->kfse", selects, flat, precision=HIGH)
    shaped = (vecs, fields, 25) + dims
    pairs = []
    for axis in range(3):
        minus = faces[:, :, 50 * axis : 50 * axis + 25].reshape(shaped)
        plus = faces[:, :, 50 * axis + 25 : 50 * axis + 50].reshape(shaped)
        pairs.append((minus, plus))
    neighbours = []
    stacks = [jnp.stack([pairs[axis][0], pairs[axis][1]], 0) for axis in range(3)]
    outer = [
        with_halo(stacks[0], (("gx", 4),), 1),
        with_halo(stacks[1], (("gy", 5),), 1),
        with_halo(stacks[2], (("gz", 6),), 1),
    ]
    for axis in range(3):
        count = dims[axis]
        after = lax.slice_in_dim(outer[axis][0], 2, count + 2, axis=3 + axis)
        before = lax.slice_in_dim(outer[axis][1], 0, count, axis=3 + axis)
        neighbours.append((after, before))
    terms = []
    for axis in range(3):
        minus, plus = pairs[axis]
        tau = penalty[axis][None, :, None, None, None, None]
        terms.append((tau * (minus - neighbours[axis][1])).reshape(vecs, fields, 25, elements))
        terms.append((tau * (plus - neighbours[axis][0])).reshape(vecs, fields, 25, elements))
    stacked = jnp.concatenate(terms, axis=2)
    return output + jnp.einsum("sq,kfse->kfqe", selects, stacked, precision=HIGH)


def precondition(flat, local_kron, element_field_factor, onehot, coarse_inverse):
    vecs, fields, elements = (flat.shape[0], flat.shape[1], flat.shape[3])
    fine = jnp.einsum("qp,kfpe->kfqe", local_kron, flat, precision=HIGH)
    fine = jnp.einsum("fg,kgqe->kfqe", element_field_factor, fine, precision=HIGH)
    nagg = coarse_inverse.shape[1] // fields
    means = jnp.sum(flat, axis=2) * (1.0 / 125.0)
    block = means.reshape(vecs * fields, elements)
    partial_sum = jnp.dot(block, onehot, precision=HIGH)
    restricted = lax.psum(partial_sum, ("gy", "gz"))
    merged = restricted.reshape(vecs, fields * nagg)
    owned = jnp.einsum("kc,rc->kr", merged, coarse_inverse, precision=HIGH)
    coarse = lax.all_gather(owned, ("gy", "gz"), axis=1, tiled=True)
    values = jnp.dot(coarse.reshape(vecs * fields, nagg), onehot.T, precision=HIGH)
    back = values.reshape(vecs, fields, elements)
    return fine + back[:, :, None, :]


def on_device(
    vectors, stiffness, flux, penalty, local_factor, element_field_factor, aggregate, coarse_inverse
):
    big = operator_matrix(stiffness, flux)
    local_kron = kron_three(local_factor, local_factor, local_factor)
    selects = jnp.asarray(face_table())
    dims = tuple(vectors.shape[3:])
    elements = aggregate.size
    nagg = coarse_inverse.shape[1] // vectors.shape[1]
    onehot = (
        aggregate.reshape(elements)[:, None] == jnp.arange(nagg, dtype=jnp.int32)[None, :]
    ).astype(jnp.float32)
    flat = vectors.reshape(vectors.shape[:3] + (elements,))
    for turn in range(2):
        flat = precondition(flat, local_kron, element_field_factor, onehot, coarse_inverse)
        flat = operate(flat, dims, big, penalty, selects)
    return flat.reshape(vectors.shape)


def solution(mesh):
    placed = (
        P(None, None, None, "gx", "gy", "gz"),
        P(),
        P(),
        P(),
        P(),
        P(),
        P("gx", "gy", "gz"),
        P(("gx", "gy", "gz"), None),
    )
    return jax.shard_map(
        on_device,
        mesh=mesh,
        in_specs=placed,
        out_specs=P(None, None, None, "gx", "gy", "gz"),
        check_vma=False,
    )
```

profile of v0, /device:TPU:225, one launch (start us, length us, event | category | flops | bytes accessed | tf_op | source)
XLA Modules:
  0.0 1826.5 jit_solution(4462123117621494507)
XLA Ops:
  6.5 2.1 reduce_sum.18
  10.7 1.7 broadcast_multiply_fusion.3
  12.3 2.8 reshape.385
  15.1 2.5 convolution_bitcast_fusion.3
  18.1 1.7 broadcast_multiply_fusion
  19.8 2.6 broadcast_multiply_fusion.2
  23.6 3.4 mul.353
  27.0 3.4 mul.364
  30.4 3.4 mul.374
  34.4 687.8 %all-reduce.3.cloned.1.call-done = f32[4,5120]{1,0:T(4,128)} async-done(((f32[4,5120]{1,0:T(4,128)}), f32[4,5120]{1,0:T(4,128)}) %all-reduce.3.cloned.1.call-update) | async-done | bytes 81936 | tf_op jit(solution)/shard_map/psum | solution.py:97
  722.2 2.3 convolution_bitcast_fusion.5
  724.4 117.8 %all-gather = f32[64,80,4]{1,2,0:T(4,128)S(1)} all-gather(f32[1,80,4]{1,2,0:T(4,128)S(1)} %convolution_bitcast_fusion.5), channel_id=1, replica_groups=mesh['gx'=4,'gy'=8,'gz'=8] {'gy','gz'}, dimensions={0}, use_global_device_ids=true | all-gather | bytes 83200 | tf_op jit(solution)/shard_map/all_gather | solution.py:100
  842.9 2.5 bitcast_add_fusion.5
  845.4 1.3 copy-done.3
  846.8 1.6 convolution_bitcast_fusion.1
  850.6 1.9 collective-permute-start.2
  852.5 9.4 collective-permute-start.3
  861.9 1.3 slice_maximum_fusion.1
  863.2 2.0 copy.64
  865.2 1.9 collective-permute-start.4
  867.1 2.0 copy.65
  869.1 2.5 collective-permute-start.5
  871.7 2.1 fusion.75
  874.9 1.3 collective-permute-start
  876.3 4.6 fusion.9
  880.9 5.0 collective-permute-start.1
  885.8 1.2 copy.66
  887.1 1.9 copy.67
  889.0 2.1 pad_maximum_fusion.4
  891.2 1.2 copy.62
  893.5 2.8 collective-permute-done
  900.3 1.3 fusion.55
  901.6 9.2 concatenate.27
  910.8 2.4 fusion.78
  913.2 4.3 fusion.76
  918.6 3.8 convolution_bitcast_fusion.2
  922.4 1.8 copy.70
  924.2 700.6 %all-reduce.5.cloned.1.call-done = f32[4,5120]{1,0:T(4,128)} async-done(((f32[4,5120]{1,0:T(4,128)}), f32[4,5120]{1,0:T(4,128)}) %all-reduce.5.cloned.1.call-update) | async-done | bytes 81936 | tf_op jit(solution)/shard_map/psum | solution.py:97
  1624.9 2.3 convolution_bitcast_fusion.4
  1627.1 118.0 %all-gather.1 = f32[64,80,4]{1,2,0:T(4,128)S(1)} all-gather(f32[1,80,4]{1,2,0:T(4,128)S(1)} %convolution_bitcast_fusion.4), channel_id=1, replica_groups=mesh['gx'=4,'gy'=8,'gz'=8] {'gy','gz'}, dimensions={0}, use_global_device_ids=true | all-gather | bytes 83200 | tf_op jit(solution)/shard_map/all_gather | solution.py:100
  1745.8 3.5 bitcast_add_fusion.2
  1749.3 1.3 copy-done.2
  1750.6 1.6 convolution_bitcast_fusion
  1752.5 1.1 copy.80
  1753.7 1.9 collective-permute-start.8
  1755.6 9.4 collective-permute-start.9
  1766.2 1.3 collective-permute-start.6
  1767.5 1.3 slice_maximum_fusion
  1768.8 1.4 copy.84
  1770.2 1.9 collective-permute-start.10
  1772.1 1.4 copy.85
  1773.6 2.4 collective-permute-start.11
  1776.0 6.2 fusion.12
  1782.2 5.0 collective-permute-start.7
  1787.1 1.2 copy.86
  1788.3 1.2 copy.87
  1789.6 2.0 pad_maximum_fusion.5
  1793.9 5.4 collective-permute-done.6
  1802.9 1.2 fusion.42
  1804.1 3.3 concatenate.31
  1807.5 4.3 fusion.79
  1811.7 1.8 copy.88
  1813.6 3.6 fusion
  1817.2 2.4 copy.89
  (143 shorter events, 22.4 us)
Async XLA Ops:
  6.5 715.7 %copy-start = (f32[80,5120]{1,0:T(8,128)S(1)}, f32[80,5120]{1,0:T(8,128)}, u32[]{:S(2)}) copy-start(f32[80,5120]{1,0:T(8,128)} %param.16) | copy-start | bytes 4915204
  6.5 3.9 copy-start.22
  6.5 715.7 %all-reduce.3.cloned.1.call-start = ((), (), s32[]{:S(2)}) async-start(), calls=%async_computation | async-start | bytes 163840 | tf_op jit(solution)/shard_map/psum | solution.py:97
  10.4 1614.5 %all-reduce.5.cloned.1.call-start = ((), (), s32[]{:S(2)}) async-start(), calls=%async_computation.1 | async-start | bytes 163840 | tf_op jit(solution)/shard_map/psum | solution.py:97
  15.1 3.0 copy-start.14
  15.1 2.6 copy-start.23
  15.1 2.9 copy-start.27
  19.8 3.2 copy-start.36
  23.6 876.7 %copy-start.25 = (f32[5]{0:T(128)}, f32[5]{0:T(128)S(1)}, u32[]{:S(2)}) copy-start(f32[5]{0:T(128)S(1)} %get-tuple-element.63) | copy-start | bytes 64
  23.6 876.7 %copy-start.28 = (f32[5]{0:T(128)}, f32[5]{0:T(128)S(1)}, u32[]{:S(2)}) copy-start(f32[5]{0:T(128)S(1)} %get-tuple-element.62) | copy-start | bytes 64
  33.8 808.6 %copy-start.37 = (s32[1,1,128]{2,1,0:T(1,128)S(1)}, s32[1,1,128]{2,1,0:T(1,128)}, u32[]{:S(2)}) copy-start(s32[1,1,128]{2,1,0:T(1,128)} %param.15) | copy-start | bytes 1540
  33.9 809.0 %copy-start.24 = (f32[5,5]{1,0:T(8,128)S(1)}, f32[5,5]{1,0:T(8,128)}, u32[]{:S(2)}) copy-start(f32[5,5]{1,0:T(8,128)} %param.14) | copy-start | bytes 304
  842.9 3.9 copy-start.12
  845.4 1.3 copy-start.3
  849.4 13.8 copy-start.6
  849.4 13.8 copy-start.9
  849.4 13.8 copy-start.10
  850.6 40.6 %collective-permute-start.2 = (f32[2,4,5,25,1,1,128]{6,1,5,4,3,2,0:T(4,128)}, f32[2,4,5,25,1,1,128]{6,1,5,4,3,2,0:T(4,128)}, u32[]{:S(2)}, u32[]{:S(2)}) collective-permute-start(f32[2,4,5,25,1,1,128]{6,1,5,4,3,2,0:T(4,128)} %copy.60), channel_id=1, source_target_pairs={{0,8},{8,16},{16,24},{24,32},{32,40},{40,48},{48,56},{1,9},{9,17},... | collective-permute-start | bytes 1536008 | tf_op jit(solution)/shard_map/ppermute | solution.py:17
  852.5 39.8 %collective-permute-start.3 = (f32[2,4,5,25,1,1,128]{6,1,5,4,3,2,0:T(4,128)}, f32[2,4,5,25,1,1,128]{6,1,5,4,3,2,0:T(4,128)}, u32[]{:S(2)}, u32[]{:S(2)}) collective-permute-start(f32[2,4,5,25,1,1,128]{6,1,5,4,3,2,0:T(4,128)} %copy.60), channel_id=1, source_target_pairs={{8,0},{16,8},{24,16},{32,24},{40,32},{48,40},{56,48},{9,1},{17,9},... | collective-permute-start | bytes 1536008 | tf_op jit(solution)/shard_map/ppermute | solution.py:18
  865.2 15.7 collective-permute-start.4
  869.1 7.1 copy-start.4
  869.1 7.1 copy-start.16
  869.1 7.1 copy-start.18
  869.1 7.1 copy-start.20
  869.1 7.1 copy-start.32
  869.1 7.1 copy-start.34
  869.1 7.1 copy-start.35
  869.1 17.9 collective-permute-start.5
  874.9 21.4 %collective-permute-start = (f32[2,4,5,25,1,1,128]{6,1,5,4,3,2,0:T(4,128)}, f32[2,4,5,25,1,1,128]{6,1,5,4,3,2,0:T(4,128)}, u32[]{:S(2)}, u32[]{:S(2)}) collective-permute-start(f32[2,4,5,25,1,1,128]{6,1,5,4,3,2,0:T(4,128)} %copy.54), channel_id=1, source_target_pairs={{0,64},{64,128},{128,192},{1,65},{65,129},{129,193},{2,66},{66,130... | collective-permute-start | bytes 1536008 | tf_op jit(solution)/shard_map/ppermute | solution.py:17
  880.9 17.0 collective-permute-start.1
  891.1 6.2 copy-start.7
  897.6 1.4 copy-start.11
  899.2 1.1 copy-start.30
  910.8 2.4 copy-start.5
  913.2 4.3 copy-start.38
  913.2 5.3 copy-start.15
  1745.8 4.8 copy-start.13
  1749.3 1.3 copy-start.2
  1752.5 15.0 copy-start.8
  1753.7 38.0 %collective-permute-start.8 = (f32[2,4,5,25,1,1,128]{6,1,5,4,3,2,0:T(4,128)}, f32[2,4,5,25,1,1,128]{6,1,5,4,3,2,0:T(4,128)}, u32[]{:S(2)}, u32[]{:S(2)}) collective-permute-start(f32[2,4,5,25,1,1,128]{6,1,5,4,3,2,0:T(4,128)} %copy.80), channel_id=1, source_target_pairs={{0,8},{8,16},{16,24},{24,32},{32,40},{40,48},{48,56},{1,9},{9,17},... | collective-permute-start | bytes 1536008 | tf_op jit(solution)/shard_map/ppermute | solution.py:17
  1755.6 37.2 %collective-permute-start.9 = (f32[2,4,5,25,1,1,128]{6,1,5,4,3,2,0:T(4,128)}, f32[2,4,5,25,1,1,128]{6,1,5,4,3,2,0:T(4,128)}, u32[]{:S(2)}, u32[]{:S(2)}) collective-permute-start(f32[2,4,5,25,1,1,128]{6,1,5,4,3,2,0:T(4,128)} %copy.80), channel_id=1, source_target_pairs={{8,0},{16,8},{24,16},{32,24},{40,32},{48,40},{56,48},{9,1},{17,9},... | collective-permute-start | bytes 1536008 | tf_op jit(solution)/shard_map/ppermute | solution.py:18
  1766.2 33.2 %collective-permute-start.6 = (f32[2,4,5,25,1,1,128]{6,1,5,4,3,2,0:T(4,128)}, f32[2,4,5,25,1,1,128]{6,1,5,4,3,2,0:T(4,128)}, u32[]{:S(2)}, u32[]{:S(2)}) collective-permute-start(f32[2,4,5,25,1,1,128]{6,1,5,4,3,2,0:T(4,128)} %copy.75), channel_id=1, source_target_pairs={{0,64},{64,128},{128,192},{1,65},{65,129},{129,193},{2,66},{66,130... | collective-permute-start | bytes 1536008 | tf_op jit(solution)/shard_map/ppermute | solution.py:17
  1767.5 8.5 copy-start.17
  1767.5 8.5 copy-start.19
  1767.5 8.5 copy-start.21
  1767.5 8.5 copy-start.33
  1770.2 11.9 collective-permute-start.10
  1773.6 14.8 collective-permute-start.11
  1782.2 18.7 %collective-permute-start.7 = (f32[2,4,5,25,1,1,128]{6,1,5,4,3,2,0:T(4,128)}, f32[2,4,5,25,1,1,128]{6,1,5,4,3,2,0:T(4,128)}, u32[]{:S(2)}, u32[]{:S(2)}) collective-permute-start(f32[2,4,5,25,1,1,128]{6,1,5,4,3,2,0:T(4,128)} %copy.75), channel_id=1, source_target_pairs={{64,0},{128,64},{192,128},{65,1},{129,65},{193,129},{66,2},{130,66... | collective-permute-start | bytes 1536008 | tf_op jit(solution)/shard_map/ppermute | solution.py:18
  1802.2 0.6 copy-start.26
  1802.2 0.7 copy-start.29
  1802.3 0.7 copy-start.31
  1813.6 6.0 copy-start.1
Sparse Core Ops, SparseCore 0:
  10.5 711.6 all-reduce.2
  918.7 706.1 all-reduce.4
where the time goes:
time: 1840 us; the launch traced here: 1830 us
  waiting for transfers between devices  1400 us (76%)
  blocking collectives  236 us (13%)
  local copies, waits for them, and re-layouts  67.1 us (4%)
  starting transfers between devices  43.9 us (2%)
  matrix products  39.6 us (2%)
  other arithmetic  29 us (2%)
    psum x2, waiting for transfers between devices, precondition(): restricted = lax.psum(partial_sum, ('gy', 'gz'))  1390 us
    all_gather x2, blocking collectives, precondition(): coarse = lax.all_gather(owned, ('gy', 'gz'), axis=1, tiled=True)  236 us
  transfers between devices with their start and end apart: 14, of which 4 were waited for; matrix products, arithmetic and copies ran while one was open for 4% of the time, Pallas kernels for 0%

commit v1 on v0

--- a/solution.py
+++ b/solution.py
@@ -94,7 +94,7 @@
     means = jnp.sum(flat, axis=2) * (1.0 / 125.0)
     block = means.reshape(vecs * fields, elements)
     partial_sum = jnp.dot(block, onehot, precision=HIGH)
-    restricted = lax.psum(partial_sum, ("gy", "gz"))
+    restricted = jnp.sum(lax.all_gather(partial_sum, ("gy", "gz")), axis=0)
     merged = restricted.reshape(vecs, fields * nagg)
     owned = jnp.einsum("kc,rc->kr", merged, coarse_inverse, precision=HIGH)
     coarse = lax.all_gather(owned, ("gy", "gz"), axis=1, tiled=True)

time: 1840 us -> 624 us (0.34)
  the two profiles are of different devices: /device:TPU:225 before, /device:TPU:33 now
where the time goes in v1:
time: 624 us; the launch traced here: 615 us
  blocking collectives  222 us (36%)
  waiting for transfers between devices  198 us (32%)
  local copies, waits for them, and re-layouts  74.9 us (12%)
  matrix products  41.1 us (7%)
  other arithmetic  36.2 us (6%)
  starting transfers between devices  28 us (4%)
  between operations  14.5 us (2%)
    all_gather x2, blocking collectives, precondition(): coarse = lax.all_gather(owned, ('gy', 'gz'), axis=1, tiled=True)  222 us
    all_gather x2, waiting for transfers between devices, precondition(): restricted = jnp.sum(lax.all_gather(partial_sum, ('gy', 'gz')), axis=0)  170 us
    ppermute x6, waiting for transfers between devices, with_halo(): after = lax.ppermute(initial, axis, down)  21.8 us
    concatenate x2, local copies, waits for them, and re-layouts, operate(): stacked = jnp.concatenate(terms, axis=2)  18.4 us
    ppermute x6, starting transfers between devices, with_halo(): before = lax.ppermute(last, axis, up)  14.9 us
    mul x8, local copies, waits for them, and re-layouts, kron_three(): return jnp.kron(jnp.kron(first, second), third)  13.4 us
    ppermute x6, starting transfers between devices, with_halo(): after = lax.ppermute(initial, axis, down)  13.1 us
  transfers between devices with their start and end apart: 14, of which 5 were waited for; matrix products, arithmetic and copies ran while one was open for 12% of the time, Pallas kernels for 0%

profile of v1, /device:TPU:33, one launch (start us, length us, event | category | flops | bytes accessed | tf_op | source)
XLA Modules:
  0.0 615.0 jit_solution(12993849464196796539)
XLA Ops:
  6.5 2.1 reduce_sum.36
  8.7 1.6 convolution_bitcast_fusion.5
  11.4 1.7 broadcast_multiply_fusion.3
  13.1 2.8 reshape.393
  16.1 2.7 broadcast_multiply_fusion.2
  18.8 3.4 mul.353
  22.2 3.4 mul.364
  25.8 1.7 broadcast_multiply_fusion
  27.5 3.4 mul.374
  32.6 2.5 convolution_bitcast_fusion.3
  35.1 80.0 %all-gather.9.cloned.1.call-done = f32[64,20,1024]{2,1,0:T(8,128)} async-done(((f32[1,20,1024]{2,1,0:T(8,128)}), f32[64,20,1024]{2,1,0:T(8,128)}) %all-gather.9.cloned.1.call-update) | async-done | bytes 5242896 | tf_op jit(solution)/shard_map/all_gather | solution.py:97
  115.1 3.2 reduce_sum.37
  118.4 1.4 convolution_bitcast_fusion.7
  119.8 111.1 %all-gather.3 = f32[64,80,4]{1,2,0:T(4,128)S(1)} all-gather(f32[1,80,4]{1,2,0:T(4,128)S(1)} %convolution_bitcast_fusion.7), channel_id=1, replica_groups=mesh['gx'=4,'gy'=8,'gz'=8] {'gy','gz'}, dimensions={0}, use_global_device_ids=true | all-gather | bytes 83200 | tf_op jit(solution)/shard_map/all_gather | solution.py:100
  231.6 2.5 bitcast_add_fusion.5
  234.1 1.3 copy-done.2
  235.5 1.6 convolution_bitcast_fusion.1
  239.3 2.1 collective-permute-start.2
  241.4 1.3 collective-permute-start.3
  242.7 1.3 slice_maximum_fusion.1
  243.9 2.0 copy.64
  246.0 1.9 collective-permute-start.4
  247.9 2.0 copy.65
  249.9 2.5 collective-permute-start.5
  252.5 2.1 fusion.73
  255.7 3.5 collective-permute-start
  259.2 4.6 fusion.9
  263.8 2.8 collective-permute-start.1
  267.9 1.9 copy.67
  269.8 2.1 pad_maximum_fusion.4
  274.3 6.3 %collective-permute-done = f32[2,4,5,25,1,1,128]{6,1,5,4,3,2,0:T(4,128)} collective-permute-done((f32[2,4,5,25,1,1,128]{6,1,5,4,3,2,0:T(4,128)}, f32[2,4,5,25,1,1,128]{6,1,5,4,3,2,0:T(4,128)}, u32[]{:S(2)}, u32[]{:S(2)}) %collective-permute-start) | collective-permute-done | bytes 512032 | tf_op jit(solution)/shard_map/ppermute | solution.py:17
  282.2 7.4 %collective-permute-done.1 = f32[2,4,5,25,1,1,128]{6,1,5,4,3,2,0:T(4,128)} collective-permute-done((f32[2,4,5,25,1,1,128]{6,1,5,4,3,2,0:T(4,128)}, f32[2,4,5,25,1,1,128]{6,1,5,4,3,2,0:T(4,128)}, u32[]{:S(2)}, u32[]{:S(2)}) %collective-permute-start.1) | collective-permute-done | bytes 512032 | tf_op jit(solution)/shard_map/ppermute | solution.py:18
  292.0 1.3 fusion.53
  293.4 9.2 %concatenate.27 = f32[4,5,150,128]{3,2,1,0:T(8,128)S(1)} concatenate(f32[4,5,25,128]{3,2,1,0:T(8,128)} %fusion.63, f32[4,5,25,128]{3,2,1,0:T(8,128)} %get-tuple-element.35, f32[4,5,25,128]{3,2,1,0:T(8,128)} %get-tuple-element.36, f32[4,5,25,128]{3,2,1,0:T(8,128)} %get-tuple-element.37, f32[4,5,25,128]{3,2,1,0:T(8,128)} %get-tuple-element.22, f32[4,5,25,128]{3,2,1,0:T(8,128)S(1)} %get-tuple-element.21), dimensions={2} | concatenate | bytes 3072000 | tf_op jit(solution)/shard_map/concatenate | solution.py:85
  302.6 2.4 fusion.76
  305.0 4.3 fusion.74
  310.3 3.8 convolution_bitcast_fusion.2
  314.1 1.9 copy.70
  316.0 89.7 %all-gather.11.cloned.1.call-done = f32[64,20,1024]{2,1,0:T(8,128)} async-done(((f32[1,20,1024]{2,1,0:T(8,128)}), f32[64,20,1024]{2,1,0:T(8,128)}) %all-gather.11.cloned.1.call-update) | async-done | bytes 5242896 | tf_op jit(solution)/shard_map/all_gather | solution.py:97
  405.7 3.2 reduce_sum.39
  409.0 1.4 convolution_bitcast_fusion.6
  410.4 111.3 %all-gather.5 = f32[64,80,4]{1,2,0:T(4,128)S(1)} all-gather(f32[1,80,4]{1,2,0:T(4,128)S(1)} %convolution_bitcast_fusion.6), channel_id=1, replica_groups=mesh['gx'=4,'gy'=8,'gz'=8] {'gy','gz'}, dimensions={0}, use_global_device_ids=true | all-gather | bytes 83200 | tf_op jit(solution)/shard_map/all_gather | solution.py:100
  522.4 3.5 bitcast_add_fusion.2
  525.9 1.3 copy-done.1
  527.2 1.6 convolution_bitcast_fusion
  529.2 1.4 copy.80
  530.5 2.1 collective-permute-start.8
  532.6 1.3 collective-permute-start.9
  535.1 3.4 collective-permute-start.6
  539.9 2.0 copy.84
  541.9 1.9 collective-permute-start.10
  543.8 2.0 copy.85
  545.9 2.4 collective-permute-start.11
  548.3 6.2 %fusion.12 = f32[4,128,5,125]{1,3,2,0:T(8,128)} fusion(f32[4,5,125,128,1]{3,1,2,0,4:T(8,128)} %bitcast.224, f32[125,125]{1,0:T(8,128)} %mul.374, f32[5,5]{1,0:T(8,128)S(1)} %copy-done.33, f32[125,125]{1,0:T(8,128)} %mul.364, f32[5,5]{1,0:T(8,128)} %get-tuple-element.66, f32[125,125]{1,0:T(8,128)} %mul.353, f32[5,5]{1,0:T(8,128)} %bitcast.228), kind=kOutput, calls=%fused_computation.23 | convolution fusion | flops 2401953024 | bytes 2747800 | tf_op jit(solution)/shard_map/fqgp,kgpe->kfqe/dot_general | solution.py:59
  554.4 2.8 collective-permute-start.7
  558.4 1.9 copy.87
  560.3 2.1 pad_maximum_fusion.5
  566.5 14.4 %collective-permute-done.7 = f32[2,4,5,25,1,1,128]{6,1,5,4,3,2,0:T(4,128)} collective-permute-done((f32[2,4,5,25,1,1,128]{6,1,5,4,3,2,0:T(4,128)}, f32[2,4,5,25,1,1,128]{6,1,5,4,3,2,0:T(4,128)}, u32[]{:S(2)}, u32[]{:S(2)}) %collective-permute-start.7) | collective-permute-done | bytes 512032 | tf_op jit(solution)/shard_map/ppermute | solution.py:18
  582.8 1.4 fusion.40
  584.2 9.2 %concatenate.31 = f32[4,5,150,128]{3,2,1,0:T(8,128)S(1)} concatenate(f32[4,5,25,128]{3,2,1,0:T(8,128)} %get-tuple-element.25, f32[4,5,25,128]{3,2,1,0:T(8,128)} %get-tuple-element.26, f32[4,5,25,128]{3,2,1,0:T(8,128)} %get-tuple-element.27, f32[4,5,25,128]{3,2,1,0:T(8,128)} %get-tuple-element.28, f32[4,5,25,128]{3,2,1,0:T(8,128)} %get-tuple-element.16, ...), dimensions={2} | concatenate | bytes 3072000 | tf_op jit(solution)/shard_map/concatenate | solution.py:85
  593.4 6.2 %fusion.77 = f32[4,5,128,125]{3,2,1,0:T(8,128)} fusion(f32[4,5,150,128]{3,2,1,0:T(8,128)S(1)} %concatenate.31, f32[150,125,1,1]{1,0,3,2:T(8,128)} %constant.10), kind=kOutput, calls=%fused_computation.153 | convolution fusion | flops 576000000 | bytes 2891000 | tf_op jit(solution)/shard_map/sq,kfse->kfqe/dot_general | solution.py:86
  599.6 2.9 copy.88
  602.5 3.1 fusion
  605.6 2.4 copy.89
  (145 shorter events, 26.2 us)
Async XLA Ops:
  6.5 111.9 %copy-start = (f32[80,5120]{1,0:T(8,128)S(1)}, f32[80,5120]{1,0:T(8,128)}, u32[]{:S(2)}) copy-start(f32[80,5120]{1,0:T(8,128)} %param.16) | copy-start | bytes 4915204
  6.5 4.8 copy-start.26
  6.5 108.6 %all-gather.9.cloned.1.call-start = ((), (), s32[]{:S(2)}) async-start(), calls=%async_computation | async-start | bytes 6389760 | tf_op jit(solution)/shard_map/all_gather | solution.py:97
  10.4 395.4 %all-gather.11.cloned.1.call-start = ((), (), s32[]{:S(2)}) async-start(), calls=%async_computation.1 | async-start | bytes 6389760 | tf_op jit(solution)/shard_map/all_gather | solution.py:97
  11.4 4.5 copy-start.27
  15.9 16.7 %copy-start.21 = (f32[125,125,1,1]{1,0,2,3:T(8,128)}, f32[125,125,1,1]{1,0,2,3:T(8,128)S(1)}, u32[]{:S(2)}) copy-start(f32[125,125,1,1]{1,0,2,3:T(8,128)S(1)} %reshape.393) | copy-start | bytes 187504
  25.7 5.2 copy-start.29
  25.8 5.8 copy-start.36
  118.4 112.8 %copy-start.37 = (s32[1,1,128]{2,1,0:T(1,128)S(1)}, s32[1,1,128]{2,1,0:T(1,128)}, u32[]{:S(2)}) copy-start(s32[1,1,128]{2,1,0:T(1,128)} %param.15) | copy-start | bytes 1540
  118.4 113.2 %copy-start.28 = (f32[5,5]{1,0:T(8,128)S(1)}, f32[5,5]{1,0:T(8,128)}, u32[]{:S(2)}) copy-start(f32[5,5]{1,0:T(8,128)} %param.14) | copy-start | bytes 304
  231.6 3.9 copy-start.19
  234.1 1.3 copy-start.2
  238.1 5.9 copy-start.11
  238.1 5.9 copy-start.15
  238.1 5.9 copy-start.16
  239.3 32.7 %collective-permute-start.2 = (f32[2,4,5,25,1,1,128]{6,1,5,4,3,2,0:T(4,128)}, f32[2,4,5,25,1,1,128]{6,1,5,4,3,2,0:T(4,128)}, u32[]{:S(2)}, u32[]{:S(2)}) collective-permute-start(f32[2,4,5,25,1,1,128]{6,1,5,4,3,2,0:T(4,128)} %copy.60), channel_id=1, source_target_pairs={{0,8},{8,16},{16,24},{24,32},{32,40},{40,48},{48,56},{1,9},{9,17},... | collective-permute-start | bytes 1536008 | tf_op jit(solution)/shard_map/ppermute | solution.py:17
  241.4 31.8 %collective-permute-start.3 = (f32[2,4,5,25,1,1,128]{6,1,5,4,3,2,0:T(4,128)}, f32[2,4,5,25,1,1,128]{6,1,5,4,3,2,0:T(4,128)}, u32[]{:S(2)}, u32[]{:S(2)}) collective-permute-start(f32[2,4,5,25,1,1,128]{6,1,5,4,3,2,0:T(4,128)} %copy.60), channel_id=1, source_target_pairs={{8,0},{16,8},{24,16},{32,24},{40,32},{48,40},{56,48},{9,1},{17,9},... | collective-permute-start | bytes 1536008 | tf_op jit(solution)/shard_map/ppermute | solution.py:18
  246.0 17.9 %collective-permute-start.4 = (f32[2,4,5,25,1,1,1]{3,1,6,5,4,2,0:T(4,128)}, f32[2,4,5,25,1,1,1]{3,1,6,5,4,2,0:T(4,128)S(1)}, u32[]{:S(2)}, u32[]{:S(2)}) collective-permute-start(f32[2,4,5,25,1,1,1]{3,1,6,5,4,2,0:T(4,128)} %copy.64), channel_id=1, source_target_pairs={{0,1},{1,2},{2,3},{3,4},{4,5},{5,6},{6,7},{8,9},{9,10},{10,11},{11... | collective-permute-start | bytes 12008 | tf_op jit(solution)/shard_map/ppermute | solution.py:17
  249.9 9.3 %copy-start.3 = (f32[4,5,125,128]{3,1,2,0:T(8,128)S(1)}, f32[4,5,125,128]{3,1,2,0:T(8,128)}, u32[]{:S(2)}) copy-start(f32[4,5,125,128]{3,1,2,0:T(8,128)} %copy-done.2) | copy-start | bytes 3840004
  249.9 9.3 %copy-start.23 = (f32[125,125]{1,0:T(8,128)S(1)}, f32[125,125]{1,0:T(8,128)}, u32[]{:S(2)}) copy-start(f32[125,125]{1,0:T(8,128)} %mul.353) | copy-start | bytes 187504
  249.9 9.3 %copy-start.24 = (f32[125,125]{1,0:T(8,128)S(1)}, f32[125,125]{1,0:T(8,128)}, u32[]{:S(2)}) copy-start(f32[125,125]{1,0:T(8,128)} %mul.364) | copy-start | bytes 187504
  249.9 9.3 %copy-start.25 = (f32[125,125]{1,0:T(8,128)S(1)}, f32[125,125]{1,0:T(8,128)}, u32[]{:S(2)}) copy-start(f32[125,125]{1,0:T(8,128)} %mul.374) | copy-start | bytes 187504
  249.9 9.3 %copy-start.32 = (f32[5,5]{1,0:T(8,128)S(1)}, f32[5,5]{1,0:T(8,128)}, u32[]{:S(2)}) copy-start(f32[5,5]{1,0:T(8,128)} %get-tuple-element.65) | copy-start | bytes 304
  249.9 9.3 %copy-start.34 = (f32[5,5]{1,0:T(8,128)S(1)}, f32[5,5]{1,0:T(8,128)}, u32[]{:S(2)}) copy-start(f32[5,5]{1,0:T(8,128)} %get-tuple-element.66) | copy-start | bytes 304
  249.9 9.3 %copy-start.35 = (f32[1,5,5]{2,1,0:T(8,128)S(1)}, f32[1,5,5]{2,1,0:T(8,128)}, u32[]{:S(2)}) copy-start(f32[1,5,5]{2,1,0:T(8,128)} %copy.133) | copy-start | bytes 304
  249.9 17.9 %collective-permute-start.5 = (f32[2,4,5,25,1,1,1]{3,1,6,5,4,2,0:T(4,128)}, f32[2,4,5,25,1,1,1]{3,1,6,5,4,2,0:T(4,128)}, u32[]{:S(2)}, u32[]{:S(2)}) collective-permute-start(f32[2,4,5,25,1,1,1]{3,1,6,5,4,2,0:T(4,128)} %copy.65), channel_id=1, source_target_pairs={{1,0},{2,1},{3,2},{4,3},{5,4},{6,5},{7,6},{9,8},{10,9},{11,10},{12... | collective-permute-start | bytes 12008 | tf_op jit(solution)/shard_map/ppermute | solution.py:18
  255.7 25.0 %collective-permute-start = (f32[2,4,5,25,1,1,128]{6,1,5,4,3,2,0:T(4,128)}, f32[2,4,5,25,1,1,128]{6,1,5,4,3,2,0:T(4,128)}, u32[]{:S(2)}, u32[]{:S(2)}) collective-permute-start(f32[2,4,5,25,1,1,128]{6,1,5,4,3,2,0:T(4,128)} %copy.54), channel_id=1, source_target_pairs={{0,64},{64,128},{128,192},{1,65},{65,129},{129,193},{2,66},{66,130... | collective-permute-start | bytes 1536008 | tf_op jit(solution)/shard_map/ppermute | solution.py:17
  263.8 25.8 %collective-permute-start.1 = (f32[2,4,5,25,1,1,128]{6,1,5,4,3,2,0:T(4,128)}, f32[2,4,5,25,1,1,128]{6,1,5,4,3,2,0:T(4,128)}, u32[]{:S(2)}, u32[]{:S(2)}) collective-permute-start(f32[2,4,5,25,1,1,128]{6,1,5,4,3,2,0:T(4,128)} %copy.54), channel_id=1, source_target_pairs={{64,0},{128,64},{192,128},{65,1},{129,65},{193,129},{66,2},{130,66... | collective-permute-start | bytes 1536008 | tf_op jit(solution)/shard_map/ppermute | solution.py:18
  272.0 9.8 %copy-start.12 = (f32[1,4,5,25,1,1,128]{6,3,2,1,5,4,0:T(8,128)S(1)}, f32[1,4,5,25,1,1,128]{6,3,2,1,5,4,0:T(8,128)}, u32[]{:S(2)}) copy-start(f32[1,4,5,25,1,1,128]{6,3,2,1,5,4,0:T(8,128)} %copy-done.11) | copy-start | bytes 768004
  282.0 8.8 %copy-start.17 = (f32[2,4,5,25,1,1,128]{6,3,2,1,4,5,0:T(8,128)S(1)}, f32[2,4,5,25,1,1,128]{6,3,2,1,4,5,0:T(8,128)}, u32[]{:S(2)}) copy-start(f32[2,4,5,25,1,1,128]{6,3,2,1,4,5,0:T(8,128)} %get-tuple-element.52) | copy-start | bytes 1536004
  291.0 1.1 copy-start.30
  302.6 2.4 copy-start.4
  305.0 4.3 copy-start.38
  305.0 5.3 copy-start.22
  522.4 4.8 copy-start.20
  525.9 1.3 copy-start.1
  529.1 4.9 copy-start.5
  529.1 4.9 copy-start.7
  529.1 4.9 copy-start.9
  529.1 9.5 %copy-start.13 = (f32[1,4,5,25,1,1,128]{6,3,2,1,5,4,0:T(8,128)}, f32[1,4,5,25,1,1,128]{6,3,2,1,5,4,0:T(8,128)S(1)}, u32[]{:S(2)}) copy-start(f32[1,4,5,25,1,1,128]{6,3,2,1,5,4,0:T(8,128)S(1)} %get-tuple-element.29) | copy-start | bytes 768004
  529.1 9.5 %copy-start.14 = (f32[1,4,5,25,1,1,128]{6,3,2,1,5,4,0:T(8,128)}, f32[1,4,5,25,1,1,128]{6,3,2,1,5,4,0:T(8,128)S(1)}, u32[]{:S(2)}) copy-start(f32[1,4,5,25,1,1,128]{6,3,2,1,5,4,0:T(8,128)S(1)} %get-tuple-element.32) | copy-start | bytes 768004
  530.5 32.0 %collective-permute-start.8 = (f32[2,4,5,25,1,1,128]{6,1,5,4,3,2,0:T(4,128)}, f32[2,4,5,25,1,1,128]{6,1,5,4,3,2,0:T(4,128)}, u32[]{:S(2)}, u32[]{:S(2)}) collective-permute-start(f32[2,4,5,25,1,1,128]{6,1,5,4,3,2,0:T(4,128)} %copy.80), channel_id=1, source_target_pairs={{0,8},{8,16},{16,24},{24,32},{32,40},{40,48},{48,56},{1,9},{9,17},... | collective-permute-start | bytes 1536008 | tf_op jit(solution)/shard_map/ppermute | solution.py:17
  532.6 31.1 %collective-permute-start.9 = (f32[2,4,5,25,1,1,128]{6,1,5,4,3,2,0:T(4,128)}, f32[2,4,5,25,1,1,128]{6,1,5,4,3,2,0:T(4,128)}, u32[]{:S(2)}, u32[]{:S(2)}) collective-permute-start(f32[2,4,5,25,1,1,128]{6,1,5,4,3,2,0:T(4,128)} %copy.80), channel_id=1, source_target_pairs={{8,0},{16,8},{24,16},{32,24},{40,32},{48,40},{56,48},{9,1},{17,9},... | collective-permute-start | bytes 1536008 | tf_op jit(solution)/shard_map/ppermute | solution.py:18
  535.1 29.8 %collective-permute-start.6 = (f32[2,4,5,25,1,1,128]{6,1,5,4,3,2,0:T(4,128)}, f32[2,4,5,25,1,1,128]{6,1,5,4,3,2,0:T(4,128)}, u32[]{:S(2)}, u32[]{:S(2)}) collective-permute-start(f32[2,4,5,25,1,1,128]{6,1,5,4,3,2,0:T(4,128)} %copy.75), channel_id=1, source_target_pairs={{0,64},{64,128},{128,192},{1,65},{65,129},{129,193},{2,66},{66,130... | collective-permute-start | bytes 1536008 | tf_op jit(solution)/shard_map/ppermute | solution.py:17
  538.6 9.6 %copy-start.33 = (f32[5,5]{1,0:T(8,128)S(1)}, f32[5,5]{1,0:T(8,128)}, u32[]{:S(2)}) copy-start(f32[5,5]{1,0:T(8,128)} %get-tuple-element.65) | copy-start | bytes 304
  541.9 12.5 %collective-permute-start.10 = (f32[2,4,5,25,1,1,1]{3,1,6,5,4,2,0:T(4,128)}, f32[2,4,5,25,1,1,1]{3,1,6,5,4,2,0:T(4,128)S(1)}, u32[]{:S(2)}, u32[]{:S(2)}) collective-permute-start(f32[2,4,5,25,1,1,1]{3,1,6,5,4,2,0:T(4,128)} %copy.84), channel_id=1, source_target_pairs={{0,1},{1,2},{2,3},{3,4},{4,5},{5,6},{6,7},{8,9},{9,10},{10,11},{11... | collective-permute-start | bytes 12008 | tf_op jit(solution)/shard_map/ppermute | solution.py:17
  545.9 12.6 %collective-permute-start.11 = (f32[2,4,5,25,1,1,1]{3,1,6,5,4,2,0:T(4,128)}, f32[2,4,5,25,1,1,1]{3,1,6,5,4,2,0:T(4,128)}, u32[]{:S(2)}, u32[]{:S(2)}) collective-permute-start(f32[2,4,5,25,1,1,1]{3,1,6,5,4,2,0:T(4,128)} %copy.85), channel_id=1, source_target_pairs={{1,0},{2,1},{3,2},{4,3},{5,4},{6,5},{7,6},{9,8},{10,9},{11,10},{12... | collective-permute-start | bytes 12008 | tf_op jit(solution)/shard_map/ppermute | solution.py:18
  554.4 26.4 %collective-permute-start.7 = (f32[2,4,5,25,1,1,128]{6,1,5,4,3,2,0:T(4,128)}, f32[2,4,5,25,1,1,128]{6,1,5,4,3,2,0:T(4,128)}, u32[]{:S(2)}, u32[]{:S(2)}) collective-permute-start(f32[2,4,5,25,1,1,128]{6,1,5,4,3,2,0:T(4,128)} %copy.75), channel_id=1, source_target_pairs={{64,0},{128,64},{192,128},{65,1},{129,65},{193,129},{66,2},{130,66... | collective-permute-start | bytes 1536008 | tf_op jit(solution)/shard_map/ppermute | solution.py:18
  562.5 3.5 copy-start.8
  562.6 3.5 copy-start.10
  566.3 15.7 %copy-start.6 = (f32[1,4,5,25,1,1,128]{6,3,2,1,4,5,0:T(8,128)S(1)}, f32[1,4,5,25,1,1,128]{6,3,2,1,4,5,0:T(8,128)}, u32[]{:S(2)}) copy-start(f32[1,4,5,25,1,1,128]{6,3,2,1,4,5,0:T(8,128)} %copy-done.5) | copy-start | bytes 768004
  582.2 0.6 copy-start.31
  599.6 2.9 copy-start.18
Sparse Core Ops, SparseCore 0:
  11.1 104.0 all-gather.8
  310.4 95.2 all-gather.10
